TPU v7x, 512 devices: a whole 4x4x16 slice. The times are simulated.
512 devices in a mesh: head: 8 (over x, core), group: 64 (over z, y).
Axes of the slice: x: 4, y: 4, z: 16, core: 2. Of those that a mesh axis runs over, the one named last changes fastest.
Arguments:
- query_proj: bfloat16 [8192, 2048], P('group', 'head'), may hold values from -6 to 6
- key_proj: bfloat16 [8192, 2048], P('group', 'head'), may hold values from -6 to 6
- value_proj: bfloat16 [8192, 4096], P('group', 'head'), may hold values from -6 to 6
- gate_proj: bfloat16 [8192, 4096], P('group', 'head'), may hold values from -6 to 6
- log_decay: float32 [8192, 8], P('group', 'head'), may hold values from -0.75 to 0
- out_weight: bfloat16 [4096, 2048], P('head'), may hold values from -0.09375 to 0.09375
- residual: bfloat16 [64, 128, 2048], P('group', 'head'), may hold values from -30 to 30
- norm_gain: float32 [2048], replicated, may hold values from 0.5 to 1.5
- vocab_weight: bfloat16 [49152, 2048], P(('head', 'group')), may hold values from -2 to 2
- targets: int32 [64, 128], P('group', 'head'), may hold values from 0 to 49151
- ref_logp: float32 [64, 128], P('group', 'head'), may hold values from -16 to -1
- response_mask: int32 [64, 128], P('group', 'head'), may hold values 0 or 1
- seq_lengths: int32 [32], replicated, may hold values from 1 to 4096, 8192 in all
Outputs:
- seq_ratio: float32 [32], replicated
- state_norms: float32 [64, 8], P('group', 'head')
- max_logits: float32 [64, 128], P('group', 'head')
Inputs may be any that keep to these rules, and one draw needn't show every extreme that they name: `seq_lengths`: the sequences lie end to end in order from position 0, the lengths summing to 8192.
All inputs are finite; a program needn't handle non-finite values. No bound on the sum of `response_mask` on one device may be relied on, other than what follows from the above.
Results may differ from a plain program's by a relative error of at most 0.00093.
Values may be sent and summed in bfloat16 or wider, within the bound.
No kernel may reach another device: no remote copies, remote signals or barrier semaphores. Data moves between devices by JAX's collectives and lax.ppermute only.
A program may use at most 192 MiB of HBM per device.

v0:
```python
import jax
import jax.numpy as jnp
from jax import lax
from jax.sharding import PartitionSpec as P


def entering(value, axis, combine, identity):
    size, index = (lax.axis_size(axis), lax.axis_index(axis))
    everything = jax.tree.map(lambda part: lax.all_gather(part, axis), value)
    start = jax.tree.map(
        lambda part, zero: jnp.broadcast_to(jnp.asarray(zero, part.dtype), part.shape),
        value,
        identity,
    )

    def lap(k, before):
        reached = k < index
        new = combine(before, jax.tree.map(lambda part: part[k], everything))
        return jax.tree.map(lambda a, b: jnp.where(reached, a, b), new, before)

    return lax.fori_loop(0, size, lap, start)


def merged_2(part, axis, combine):
    gathered = jax.tree.map(lambda a: lax.all_gather(a, axis), part)

    def take(source):
        return jax.tree.map(lambda a: lax.dynamic_index_in_dim(a, source, 0, False), gathered)

    return lax.fori_loop(
        1, lax.axis_size(axis), lambda source, state: combine(state, take(source)), take(0)
    )


def layer_norm(stream, width_eps):
    mean_val = jnp.mean(stream, axis=-1, keepdims=True)
    centered = stream - mean_val
    var_val = jnp.mean(centered * centered, axis=-1, keepdims=True)
    return centered / jnp.sqrt(var_val + width_eps)


def combine_state(earlier, later):
    decay_first, state_first = earlier
    decay_second, state_second = later
    return (decay_first * decay_second, decay_second[:, None, None] * state_first + state_second)


def combine_totals(first, second):
    max_first, sum_first, target_first = first
    max_second, sum_second, target_second = second
    top = jnp.maximum(max_first, max_second)
    merged = sum_first * jnp.exp(max_first - top) + sum_second * jnp.exp(max_second - top)
    return (top, merged, target_first + target_second)


def per_device(
    query_proj,
    key_proj,
    value_proj,
    gate_proj,
    log_decay,
    out_weight,
    residual,
    norm_gain,
    vocab_weight,
    targets,
    ref_logp,
    response_mask,
    seq_lengths,
):
    highest_precision = lax.Precision.HIGHEST
    head_count = lax.axis_size("head")
    group_count = lax.axis_size("group")
    head_index = lax.axis_index("head")
    group_index = lax.axis_index("group")
    tok_count = query_proj.shape[0]
    heads_here = log_decay.shape[1]
    key_width = query_proj.shape[1] // heads_here
    value_width = value_proj.shape[1] // heads_here
    slice_rows = residual.shape[1]
    seq_count = seq_lengths.shape[0]
    vocab_here = vocab_weight.shape[0]
    key_scaling = key_width ** (-0.5)
    starts = jnp.cumsum(seq_lengths) - seq_lengths
    local_pos = jnp.arange(tok_count, dtype=jnp.int32)
    positions = group_index * tok_count + local_pos
    seq_ids = jnp.sum((positions[:, None] >= starts[None, 1:]).astype(jnp.int32), axis=1)
    is_start = jnp.any(positions[:, None] == starts[None, :], axis=1)
    cumulative_decay = jnp.cumsum(log_decay, axis=0)
    same_seq = (seq_ids[:, None] == seq_ids[None, :]) & (local_pos[None, :] <= local_pos[:, None])
    gap_log = cumulative_decay[:, None, :] - cumulative_decay[None, :, :]
    decay_mat = jnp.where(same_seq[:, :, None], jnp.exp(jnp.minimum(gap_log, 0.0)), 0.0)
    query_heads = query_proj.reshape(tok_count, heads_here, key_width)
    key_heads = key_proj.reshape(tok_count, heads_here, key_width)
    value_heads = value_proj.reshape(tok_count, heads_here, value_width)
    raw_scores = jnp.einsum(
        "thd,shd->tsh", query_heads, key_heads, preferred_element_type=jnp.float32
    )
    weights_in = (raw_scores * key_scaling * decay_mat).astype(jnp.bfloat16)
    in_block = jnp.einsum(
        "tsh,shv->thv", weights_in, value_heads, preferred_element_type=jnp.float32
    )
    continuation_flags = (seq_ids == seq_ids[0]) & jnp.logical_not(is_start[0])
    final_decay_weight = jnp.where(
        (seq_ids == seq_ids[-1])[:, None],
        jnp.exp(cumulative_decay[-1][None, :] - cumulative_decay),
        0.0,
    )
    key_as_float = key_heads.astype(jnp.float32)
    value_as_float = value_heads.astype(jnp.float32)
    block_total_sum = jnp.einsum(
        "ane,anl->nel",
        key_as_float * final_decay_weight[:, :, None],
        value_as_float,
        precision=highest_precision,
    )
    block_decay = jnp.where(jnp.all(continuation_flags), jnp.exp(cumulative_decay[-1]), 0.0)
    decay_prefix, carried_state = entering(
        (block_decay, block_total_sum),
        "group",
        combine_state,
        (jnp.ones_like(block_decay), jnp.zeros_like(block_total_sum)),
    )
    query_as_float = query_heads.astype(jnp.float32)
    state_contribution = (
        jnp.einsum("ugo,gow->ugw", query_as_float, carried_state, precision=highest_precision)
        * key_scaling
        * (jnp.exp(cumulative_decay) * continuation_flags[:, None].astype(jnp.float32))[:, :, None]
    )
    retained = in_block + state_contribution
    state_norms = jnp.log(
        1.0 + jnp.sqrt(jnp.mean(carried_state * carried_state, axis=(1, 2)) + 1e-06)
    )[None, :]
    normed = layer_norm(retained, 1e-06)
    gate_float = gate_proj.reshape(tok_count, heads_here, value_width).astype(jnp.float32)
    gated_out = (
        (normed * jax.nn.silu(gate_float))
        .astype(jnp.bfloat16)
        .reshape(tok_count, heads_here * value_width)
    )
    full_branch = lax.psum(
        jnp.dot(gated_out, out_weight, preferred_element_type=jnp.float32), "head"
    )
    own_branch = lax.dynamic_slice_in_dim(full_branch, head_index * slice_rows, slice_rows, 0)
    stream = residual[0].astype(jnp.float32) + own_branch
    hidden = (layer_norm(stream, 1e-05) * norm_gain).astype(jnp.bfloat16)
    vocab_rows = lax.all_gather(vocab_weight, "head", axis=0, tiled=True)
    entry_ids = (
        (jnp.arange(head_count, dtype=jnp.int32)[:, None] * group_count + group_index) * vocab_here
        + jnp.arange(vocab_here, dtype=jnp.int32)[None, :]
    ).reshape(-1)
    all_targets = lax.all_gather(targets, "group", axis=0, tiled=True).reshape(-1)
    logits = lax.dot_general(
        lax.all_gather(hidden, "group", axis=0, tiled=True),
        vocab_rows,
        (((1,), (1,)), ((), ())),
        preferred_element_type=jnp.float32,
    )
    top = jnp.max(logits, axis=1)
    exp_total = jnp.sum(jnp.exp(logits - top[:, None]), axis=1)
    picked = jnp.sum(jnp.where(entry_ids[None, :] == all_targets[:, None], logits, 0.0), axis=1)
    merged_max, merged_total, merged_target = merged_2(
        (top, exp_total, picked), "group", combine_totals
    )
    own_start = group_index * slice_rows
    own_max = lax.dynamic_slice_in_dim(merged_max, own_start, slice_rows, 0)
    own_total = lax.dynamic_slice_in_dim(merged_total, own_start, slice_rows, 0)
    own_target = lax.dynamic_slice_in_dim(merged_target, own_start, slice_rows, 0)
    token_logp = own_target - own_max - jnp.log(own_total)
    token_ratio = response_mask[0].astype(jnp.float32) * (token_logp - ref_logp[0])
    own_positions = (
        group_index * tok_count + head_index * slice_rows + jnp.arange(slice_rows, dtype=jnp.int32)
    )
    own_seq = jnp.sum((own_positions[:, None] >= starts[None, 1:]).astype(jnp.int32), axis=1)
    member = (own_seq[:, None] == jnp.arange(seq_count, dtype=jnp.int32)[None, :]).astype(
        jnp.float32
    )
    partial_sums = jnp.sum(member * token_ratio[:, None], axis=0)
    seq_total = lax.psum(partial_sums, ("head", "group"))
    seq_ratio = seq_total / seq_lengths.astype(jnp.float32)
    return (seq_ratio, state_norms, own_max[None, :])


def solution(mesh):
    placed = (
        P("group", "head"),
        P("group", "head"),
        P("group", "head"),
        P("group", "head"),
        P("group", "head"),
        P("head", None),
        P("group", "head", None),
        P(),
        P(("head", "group"), None),
        P("group", "head"),
        P("group", "head"),
        P("group", "head"),
        P(),
    )
    return jax.shard_map(
        per_device,
        mesh=mesh,
        in_specs=placed,
        out_specs=(P(), P("group", "head"), P("group", "head")),
        check_vma=False,
    )
```

profile of v0, /device:TPU:1, one launch (start us, length us, event | category | flops | bytes accessed | tf_op | source)
XLA Modules:
  0.0 1104.0 jit_solution(7736796579347406270)
XLA Ops:
  11.4 2.0 select_multiply_fusion
  13.4 2.2 fusion.19
  20.4 124.9 %all-reduce = f32[64]{0:T(128)S(1)} all-reduce(f32[64]{0:T(128)S(1)} %fusion.38), channel_id=2, replica_groups=mesh['head'=8,'group'=64] {'group'}, use_global_device_ids=true, to_apply=%add | all-reduce | flops 64 | bytes 512
  146.7 167.5 %all-gather.14.cloned.1.call-done = f32[16384,512]{1,0:T(8,128)} async-done(((f32[256,512]{1,0:T(8,128)}), f32[16384,512]{1,0:T(8,128)}) %all-gather.14.cloned.1.call-update) | async-done | bytes 33554448 | tf_op jit(solution)/shard_map/all_gather | solution.py:9
  314.2 163.2 %while.34 = (s32[]{:T(128)}, f32[1,256,512]{2,1,0:T(8,128)S(1)}, s32[]{:T(128)}, f32[64,1]{0,1:T(1,128)S(1)}, f32[64,1,256,512]{3,2,1,0:T(8,128)}, /*index=5*/s32[]{:T(128)}, s32[]{:T(128)}) while((s32[]{:T(128)}, f32[1,256,512]{2,1,0:T(8,128)S(1)}, s32[]{:T(128)}, f32[64,1]{0,1:T(1,128)S(1)}, f32[64,1,256,512]{3,2,1,0:T(8,128)}, ...), condition=%wide.region_7.8_spmd.clone, body=%wide.region_6.7_spmd.clone.sunk | while | flops 524292 | bytes 1572981 | solution.py:21
  314.7 1.9 fusion.55
  317.3 1.9 fusion.55
  319.8 1.9 fusion.55
  322.4 1.9 fusion.55
  324.9 1.9 fusion.55
  327.5 1.9 fusion.55
  330.0 1.9 fusion.55
  332.6 1.9 fusion.55
  335.1 1.9 fusion.55
  337.7 1.9 fusion.55
  340.2 1.9 fusion.55
  342.8 1.9 fusion.55
  345.3 1.9 fusion.55
  347.9 1.9 fusion.55
  350.4 1.9 fusion.55
  353.0 1.9 fusion.55
  355.5 1.9 fusion.55
  358.1 1.9 fusion.55
  480.4 72.8 %all-reduce.3.cloned.1.call-done = f32[128,2048]{1,0:T(8,128)} async-done(((f32[128,2048]{1,0:T(8,128)}), f32[128,2048]{1,0:T(8,128)}) %all-reduce.3.cloned.1.call-update) | async-done | bytes 1048592 | tf_op jit(solution)/shard_map/psum | solution.py:141
  557.2 63.4 %all-gather.5 = s32[64,1,16]{2,1,0:T(1,128)S(1)} all-gather(s32[1,1,16]{2,1,0:T(1,128)S(1)} %bitcast.113), channel_id=1, replica_groups=mesh['head'=8,'group'=64] {'group'}, dimensions={0}, use_global_device_ids=true | all-gather | bytes 4160 | tf_op jit(solution)/shard_map/all_gather | solution.py:152
  623.5 107.8 %all-gather.10.cloned.1.call-done = bf16[1024,2048]{1,0:T(8,128)(2,1)} async-done(((bf16[16,2048]{1,0:T(8,128)(2,1)}), bf16[1024,2048]{1,0:T(8,128)(2,1)}) %all-gather.10.cloned.1.call-update) | async-done | bytes 4194320 | tf_op jit(solution)/shard_map/all_gather | solution.py:154
  731.3 6.2 fusion.45
  738.3 61.6 %all-gather.3 = f32[65536]{0:T(1024)S(1)} all-gather(f32[1024]{0:T(1024)S(1)} %get-tuple-element.318), channel_id=5, replica_groups=mesh['head'=8,'group'=64] {'group'}, dimensions={0}, use_global_device_ids=true | all-gather | bytes 266240 | tf_op jit(solution)/shard_map/all_gather | solution.py:25
  800.0 62.9 %all-gather.4 = f32[65536]{0:T(1024)S(1)} all-gather(f32[1024]{0:T(1024)S(1)} %get-tuple-element.317), channel_id=6, replica_groups=mesh['head'=8,'group'=64] {'group'}, dimensions={0}, use_global_device_ids=true | all-gather | bytes 266240 | tf_op jit(solution)/shard_map/all_gather | solution.py:25
  863.0 63.5 %all-gather.2 = f32[65536]{0:T(1024)S(1)} all-gather(f32[1024]{0:T(1024)S(1)} %get-tuple-element.355), channel_id=4, replica_groups=mesh['head'=8,'group'=64] {'group'}, dimensions={0}, use_global_device_ids=true | all-gather | bytes 266240 | tf_op jit(solution)/shard_map/all_gather | solution.py:25
  926.6 5.9 while.33
  933.3 162.6 %psum.15 = f32[32]{0:T(128)S(1)} all-reduce(f32[32]{0:T(128)S(1)} %select_reduce_fusion.1), channel_id=1, replica_groups=mesh['head'=8,'group'=64] {'head','group'}, use_global_device_ids=true, to_apply=%region_19.20 | all-reduce | flops 32 | bytes 256 | tf_op jit(solution)/shard_map/psum | solution.py:179
  (437 shorter events, 150.8 us)
Async XLA Ops:
  7.2 470.9 %copy-start = (bf16[512,2048]{1,0:T(8,128)(2,1)S(1)}, bf16[512,2048]{1,0:T(8,128)(2,1)}, u32[]{:S(2)}) copy-start(bf16[512,2048]{1,0:T(8,128)(2,1)} %param.22) | copy-start | bytes 6291460
  7.2 307.0 %all-gather.14.cloned.1.call-start = ((), (), s32[]{:S(2)}) async-start(), calls=%async_computation.3 | async-start | bytes 34078720 | tf_op jit(solution)/shard_map/all_gather | solution.py:9
  15.6 537.5 %all-reduce.3.cloned.1.call-start = ((), (), s32[]{:S(2)}) async-start(), calls=%async_computation | async-start | bytes 2097152 | tf_op jit(solution)/shard_map/psum | solution.py:141
  314.2 163.2 %copy-start.2 = (bf16[128,256]{1,0:T(8,128)(2,1)S(1)}, bf16[128,256]{1,0:T(8,128)(2,1)}, u32[]{:S(2)}) copy-start(bf16[128,256]{1,0:T(8,128)(2,1)} %param.17) | copy-start | bytes 196612
  314.2 163.9 %copy-start.8 = (bf16[128,512]{1,0:T(8,128)(2,1)S(1)}, bf16[128,512]{1,0:T(8,128)(2,1)}, u32[]{:S(2)}) copy-start(bf16[128,512]{1,0:T(8,128)(2,1)} %param.20) | copy-start | bytes 393220
  477.4 75.8 %copy-start.1 = (bf16[1,16,2048]{2,1,0:T(8,128)(2,1)S(1)}, bf16[1,16,2048]{2,1,0:T(8,128)(2,1)}, u32[]{:S(2)}) copy-start(bf16[1,16,2048]{2,1,0:T(8,128)(2,1)} %param.23) | copy-start | bytes 196612
  477.8 77.5 %copy-start.3 = (f32[2048]{0:T(1024)S(1)}, f32[2048]{0:T(1024)}, u32[]{:S(2)}) copy-start(f32[2048]{0:T(1024)} %param.24) | copy-start | bytes 24580
  478.0 79.2 %copy-start.4 = (s32[1,16]{1,0:T(1,128)S(1)}, s32[1,16]{1,0:T(1,128)}, u32[]{:S(2)}) copy-start(s32[1,16]{1,0:T(1,128)} %param.26) | copy-start | bytes 196
  479.6 143.9 %all-gather.12.cloned.1.call-start = ((), (), s32[]{:S(2)}) async-start(), calls=%async_computation.2 | async-start | bytes 3538944 | tf_op jit(solution)/shard_map/all_gather | solution.py:147
  480.4 251.0 %all-gather.10.cloned.1.call-start = ((), (), s32[]{:S(2)}) async-start(), calls=%async_computation.1 | async-start | bytes 4259840 | tf_op jit(solution)/shard_map/all_gather | solution.py:154
  737.5 195.0 %copy-start.6 = (f32[1,16]{1,0:T(1,128)S(1)}, f32[1,16]{1,0:T(1,128)}, u32[]{:S(2)}) copy-start(f32[1,16]{1,0:T(1,128)} %param.27) | copy-start | bytes 196
  737.6 195.0 %copy-start.7 = (s32[1,16]{1,0:T(1,128)S(1)}, s32[1,16]{1,0:T(1,128)}, u32[]{:S(2)}) copy-start(s32[1,16]{1,0:T(1,128)} %param.28) | copy-start | bytes 196
  737.6 358.3 %copy-start.5 = (s32[32]{0:T(128)S(1)}, s32[32]{0:T(128)}, u32[]{:S(2)}) copy-start(s32[32]{0:T(128)} %param.29) | copy-start | bytes 388
Sparse Core Ops, SparseCore 0:
  15.8 298.3 all-gather.13
  479.7 73.3 all-reduce.2
  555.3 36.6 all-gather.11
  594.8 136.4 all-gather.9
where the time goes:
time: 1110 us; the launch traced here: 1100 us
  blocking collectives  539 us (49%)
  waiting for transfers between devices  349 us (31%)
  other arithmetic  139 us (13%)
  local copies, waits for them, and re-layouts  44.2 us (4%)
  between operations  16.6 us (1%)
  matrix products  11.8 us (1%)
    all_gather x3, blocking collectives, merged_2(): gathered = jax.tree.map(lambda a: lax.all_gather(a, axis), part)  188 us
    all_gather x1, waiting for transfers between devices, entering(): everything = jax.tree.map(lambda part: lax.all_gather(part, axis), value)  167 us
    psum x1, blocking collectives, per_device(): seq_total = lax.psum(partial_sums, ('head', 'group'))  163 us
    unnamed x1, blocking collectives  125 us
    select_n x64, other arithmetic, lap(): return jax.tree.map(lambda a, b: jnp.where(reached, a, b), new, before)  125 us
    all_gather x1, waiting for transfers between devices, per_device(): lax.all_gather(hidden, 'group', axis=0, tiled=True)  108 us
    psum x1, waiting for transfers between devices, per_device(): lax.psum(jnp.dot(gated_out, out_weight, preferred_element_type=jnp.float3...  72.8 us
    all_gather x1, blocking collectives, per_device(): lax.all_gather(targets, 'group', axis=0, tiled=True).reshape(-1)  63.4 us
  transfers between devices with their start and end apart: 4, of which 3 were waited for; matrix products, arithmetic and copies ran while one was open for 1% of the time, Pallas kernels for 0%

commit v1 on v0

--- a/solution.py
+++ b/solution.py
@@ -151,7 +151,9 @@
     ).reshape(-1)
     all_targets = lax.all_gather(targets, "group", axis=0, tiled=True).reshape(-1)
     logits = lax.dot_general(
-        lax.all_gather(hidden, "group", axis=0, tiled=True),
+        jnp.concatenate(
+            lax.all_to_all(jnp.stack([hidden] * lax.axis_size("group")), "group", 0, 0), axis=0
+        ),
         vocab_rows,
         (((1,), (1,)), ((), ())),
         preferred_element_type=jnp.float32,

time: 1110 us -> 1200 us (1.081)
  blocking collectives: 539 us -> 716 us
  waiting for transfers between devices: 349 us -> 242 us
  starting transfers between devices: 0.16 us -> 15.4 us
    all_gather x1, blocking collectives: 63.4 us -> 231 us  [per_device(): lax.all_gather(targets, 'group', axis=0, tiled=True).reshape(-1)]
    all_gather x1 -> x0, waiting for transfers between devices: 108 us -> none  [per_device(): lax.all_gather(hidden, 'group', axis=0, tiled=True)]
    all_to_all x0 -> x1, starting transfers between devices: none -> 15.3 us  [per_device(): lax.all_to_all(jnp.stack([hidden] * lax.axis_size('group')), 'group', 0, 0)]
  transfers between devices with their start and end apart: 4 -> 4, of which waited for: 3 -> 2; matrix products, arithmetic and copies ran while one was open for 1% -> 1% of each run, Pallas kernels for 0% -> 0%
where the time goes in v1:
time: 1200 us; the launch traced here: 1190 us
  blocking collectives  716 us (60%)
  waiting for transfers between devices  242 us (20%)
  other arithmetic  139 us (12%)
  local copies, waits for them, and re-layouts  46.7 us (4%)
  between operations  16.6 us (1%)
  starting transfers between devices  15.4 us (1%)
    all_gather x1, blocking collectives, per_device(): lax.all_gather(targets, 'group', axis=0, tiled=True).reshape(-1)  231 us
    all_gather x3, blocking collectives, merged_2(): gathered = jax.tree.map(lambda a: lax.all_gather(a, axis), part)  188 us
    psum x1, blocking collectives, per_device(): seq_total = lax.psum(partial_sums, ('head', 'group'))  172 us
    all_gather x1, waiting for transfers between devices, entering(): everything = jax.tree.map(lambda part: lax.all_gather(part, axis), value)  167 us
    unnamed x1, blocking collectives  125 us
    select_n x64, other arithmetic, lap(): return jax.tree.map(lambda a, b: jnp.where(reached, a, b), new, before)  125 us
    psum x1, waiting for transfers between devices, per_device(): lax.psum(jnp.dot(gated_out, out_weight, preferred_element_type=jnp.float3...  73.5 us
    dynamic_slice x64, local copies, waits for them, and re-layouts, lap(): new = combine(before, jax.tree.map(lambda part: part[k], everything))  37.4 us
  transfers between devices with their start and end apart: 4, of which 2 were waited for; matrix products, arithmetic and copies ran while one was open for 1% of the time, Pallas kernels for 0%

profile of v1, /device:TPU:1, one launch (start us, length us, event | category | flops | bytes accessed | tf_op | source)
XLA Modules:
  0.0 1191.1 jit_solution(15771714421257359673)
XLA Ops:
  11.4 2.0 select_multiply_fusion
  13.4 2.2 fusion.19
  20.4 124.9 %all-reduce = f32[64]{0:T(128)S(1)} all-reduce(f32[64]{0:T(128)S(1)} %fusion.38), channel_id=2, replica_groups=mesh['head'=8,'group'=64] {'group'}, use_global_device_ids=true, to_apply=%add | all-reduce | flops 64 | bytes 512
  146.7 167.5 %all-gather.11.cloned.1.call-done = f32[16384,512]{1,0:T(8,128)} async-done(((f32[256,512]{1,0:T(8,128)}), f32[16384,512]{1,0:T(8,128)}) %all-gather.11.cloned.1.call-update) | async-done | bytes 33554448 | tf_op jit(solution)/shard_map/all_gather | solution.py:9
  314.2 163.2 %while.34 = (s32[]{:T(128)}, f32[1,256,512]{2,1,0:T(8,128)S(1)}, s32[]{:T(128)}, f32[64,1]{0,1:T(1,128)S(1)}, f32[64,1,256,512]{3,2,1,0:T(8,128)}, /*index=5*/s32[]{:T(128)}, s32[]{:T(128)}) while((s32[]{:T(128)}, f32[1,256,512]{2,1,0:T(8,128)S(1)}, s32[]{:T(128)}, f32[64,1]{0,1:T(1,128)S(1)}, f32[64,1,256,512]{3,2,1,0:T(8,128)}, ...), condition=%wide.region_7.8_spmd.clone, body=%wide.region_6.7_spmd.clone.sunk | while | flops 524292 | bytes 1572981 | solution.py:21
  314.7 1.9 fusion.55
  317.3 1.9 fusion.55
  319.8 1.9 fusion.55
  322.4 1.9 fusion.55
  324.9 1.9 fusion.55
  327.5 1.9 fusion.55
  330.0 1.9 fusion.55
  332.6 1.9 fusion.55
  335.1 1.9 fusion.55
  337.7 1.9 fusion.55
  340.2 1.9 fusion.55
  342.8 1.9 fusion.55
  345.3 1.9 fusion.55
  347.9 1.9 fusion.55
  350.4 1.9 fusion.55
  353.0 1.9 fusion.55
  355.5 1.9 fusion.55
  479.6 73.5 %all-reduce.3.cloned.1.call-done = f32[128,2048]{1,0:T(8,128)} async-done(((f32[128,2048]{1,0:T(8,128)}), f32[128,2048]{1,0:T(8,128)}) %all-reduce.3.cloned.1.call-update) | async-done | bytes 1048592 | tf_op jit(solution)/shard_map/psum | solution.py:141
  556.3 2.5 stack.2
  558.8 15.3 %all-to-all-start = ((bf16[64,16,2048]{2,1,0:T(8,128)(2,1)}), bf16[64,16,2048]{2,1,0:T(8,128)(2,1)}, u32[]{:S(2)}, u32[]{:S(2)}) async-start(bf16[64,16,2048]{2,1,0:T(8,128)(2,1)} %stack.2), calls=%async_computation | async-start | bytes 8388608 | tf_op jit(solution)/shard_map/all_to_all | solution.py:155
  575.0 231.2 %all-gather.5 = s32[64,1,16]{2,1,0:T(1,128)S(1)} all-gather(s32[1,1,16]{2,1,0:T(1,128)S(1)} %bitcast.114), channel_id=1, replica_groups=mesh['head'=8,'group'=64] {'group'}, dimensions={0}, use_global_device_ids=true | all-gather | bytes 4160 | tf_op jit(solution)/shard_map/all_gather | solution.py:152
  809.2 6.2 fusion.45
  816.2 62.3 %all-gather.3 = f32[65536]{0:T(1024)S(1)} all-gather(f32[1024]{0:T(1024)S(1)} %get-tuple-element.318), channel_id=5, replica_groups=mesh['head'=8,'group'=64] {'group'}, dimensions={0}, use_global_device_ids=true | all-gather | bytes 266240 | tf_op jit(solution)/shard_map/all_gather | solution.py:25
  878.6 63.2 %all-gather.4 = f32[65536]{0:T(1024)S(1)} all-gather(f32[1024]{0:T(1024)S(1)} %get-tuple-element.317), channel_id=6, replica_groups=mesh['head'=8,'group'=64] {'group'}, dimensions={0}, use_global_device_ids=true | all-gather | bytes 266240 | tf_op jit(solution)/shard_map/all_gather | solution.py:25
  941.8 62.5 %all-gather.2 = f32[65536]{0:T(1024)S(1)} all-gather(f32[1024]{0:T(1024)S(1)} %get-tuple-element.355), channel_id=4, replica_groups=mesh['head'=8,'group'=64] {'group'}, dimensions={0}, use_global_device_ids=true | all-gather | bytes 266240 | tf_op jit(solution)/shard_map/all_gather | solution.py:25
  1004.4 5.9 while.33
  1011.1 171.8 %psum.15 = f32[32]{0:T(128)S(1)} all-reduce(f32[32]{0:T(128)S(1)} %select_reduce_fusion.1), channel_id=1, replica_groups=mesh['head'=8,'group'=64] {'head','group'}, use_global_device_ids=true, to_apply=%region_19.20 | all-reduce | flops 32 | bytes 256 | tf_op jit(solution)/shard_map/psum | solution.py:181
  (437 shorter events, 152.1 us)
Async XLA Ops:
  7.2 470.9 %copy-start = (bf16[512,2048]{1,0:T(8,128)(2,1)S(1)}, bf16[512,2048]{1,0:T(8,128)(2,1)}, u32[]{:S(2)}) copy-start(bf16[512,2048]{1,0:T(8,128)(2,1)} %param.22) | copy-start | bytes 6291460
  7.2 307.0 %all-gather.11.cloned.1.call-start = ((), (), s32[]{:S(2)}) async-start(), calls=%async_computation.3 | async-start | bytes 34078720 | tf_op jit(solution)/shard_map/all_gather | solution.py:9
  15.6 537.5 %all-reduce.3.cloned.1.call-start = ((), (), s32[]{:S(2)}) async-start(), calls=%async_computation.1 | async-start | bytes 2097152 | tf_op jit(solution)/shard_map/psum | solution.py:141
  314.2 163.2 %copy-start.2 = (bf16[128,256]{1,0:T(8,128)(2,1)S(1)}, bf16[128,256]{1,0:T(8,128)(2,1)}, u32[]{:S(2)}) copy-start(bf16[128,256]{1,0:T(8,128)(2,1)} %param.17) | copy-start | bytes 196612
  314.2 163.9 %copy-start.8 = (bf16[128,512]{1,0:T(8,128)(2,1)S(1)}, bf16[128,512]{1,0:T(8,128)(2,1)}, u32[]{:S(2)}) copy-start(bf16[128,512]{1,0:T(8,128)(2,1)} %param.20) | copy-start | bytes 393220
  477.4 75.8 %copy-start.1 = (bf16[1,16,2048]{2,1,0:T(8,128)(2,1)S(1)}, bf16[1,16,2048]{2,1,0:T(8,128)(2,1)}, u32[]{:S(2)}) copy-start(bf16[1,16,2048]{2,1,0:T(8,128)(2,1)} %param.23) | copy-start | bytes 196612
  477.4 78.0 %copy-start.3 = (f32[2048]{0:T(1024)S(1)}, f32[2048]{0:T(1024)}, u32[]{:S(2)}) copy-start(f32[2048]{0:T(1024)} %param.24) | copy-start | bytes 24580
  558.8 16.2 %copy-start.4 = (s32[1,16]{1,0:T(1,128)S(1)}, s32[1,16]{1,0:T(1,128)}, u32[]{:S(2)}) copy-start(s32[1,16]{1,0:T(1,128)} %param.26) | copy-start | bytes 196
  558.8 250.4 %all-to-all-start = ((bf16[64,16,2048]{2,1,0:T(8,128)(2,1)}), bf16[64,16,2048]{2,1,0:T(8,128)(2,1)}, u32[]{:S(2)}, u32[]{:S(2)}) async-start(bf16[64,16,2048]{2,1,0:T(8,128)(2,1)} %stack.2), calls=%async_computation | async-start | bytes 8388608 | tf_op jit(solution)/shard_map/all_to_all | solution.py:155
  574.1 235.1 %all-gather.9.cloned.1.call-start = ((), (), s32[]{:S(2)}) async-start(), calls=%async_computation.2 | async-start | bytes 3538944 | tf_op jit(solution)/shard_map/all_gather | solution.py:147
  815.5 194.9 %copy-start.6 = (f32[1,16]{1,0:T(1,128)S(1)}, f32[1,16]{1,0:T(1,128)}, u32[]{:S(2)}) copy-start(f32[1,16]{1,0:T(1,128)} %param.27) | copy-start | bytes 196
  815.5 194.9 %copy-start.7 = (s32[1,16]{1,0:T(1,128)S(1)}, s32[1,16]{1,0:T(1,128)}, u32[]{:S(2)}) copy-start(s32[1,16]{1,0:T(1,128)} %param.28) | copy-start | bytes 196
  815.5 367.4 %copy-start.5 = (s32[32]{0:T(128)S(1)}, s32[32]{0:T(128)}, u32[]{:S(2)}) copy-start(s32[32]{0:T(128)} %param.29) | copy-start | bytes 388
Sparse Core Ops, SparseCore 0:
  15.8 298.3 all-gather.10
  479.8 73.3 all-reduce.2
  577.0 36.3 all-gather.8
